TPU v7x, 256 devices: a whole 4x4x8 slice. The times are simulated.
256 devices in a mesh: seq: 64 (over x, z_lo, y, core), mp: 4 (over z_hi).
Axes of the slice: x: 4, y: 4, z: 8 (z_hi: 4, z_lo: 2; z = z_hi * 2 + z_lo), core: 2. Of those that a mesh axis runs over, the one named last changes fastest.
Arguments:
- tokens: bfloat16 [8192, 4096], P('seq', 'mp'), may hold values from -6 to 6
- w_proj: bfloat16 [4096, 3, 2048], P('seq', None, 'mp'), may hold values from -0.09375 to 0.09375
- short_filter: float32 [3, 3, 2048], P(None, None, 'mp'), may hold values from -3.5 to 3.5
- long_filter: float32 [2048, 8192], P(('mp', 'seq')), may hold values from -0.0625 to 0.0625
- skip_gain: float32 [2048], P('mp'), may hold values from -4 to 4
Outputs:
- gated: bfloat16 [8192, 2048], P('seq', 'mp')
All inputs are finite; a program needn't handle non-finite values.
Results may differ from a plain program's by a relative error of at most 0.012.
Values may be sent and summed in bfloat16 or wider, within the bound.
No kernel may reach another device: no remote copies, remote signals or barrier semaphores. Data moves between devices by JAX's collectives and lax.ppermute only.
A program may use at most 64 MiB of HBM per device.

v0:
```python
import math
import jax
import jax.numpy as jnp
from jax import lax
from jax.sharding import PartitionSpec as P


def shifted(value, axis, steps):
    count = lax.axis_size(axis)
    leading, last = (max(0, -steps), min(count, count - steps))
    return lax.ppermute(value, axis, [(source, source + steps) for source in range(leading, last)])


def transform(real_part, imag_part, orient, filled):
    length = real_part.shape[-1]
    first = math.gcd(length, 64)
    highest = lax.Precision.HIGHEST
    if length <= 64 or first == 1:
        counter = jnp.arange(length, dtype=jnp.int32)
        angles = (
            2.0
            * math.pi
            / length
            * (counter[:, None] * counter[None, :] % length).astype(jnp.float32)
        )
        cosine = jnp.cos(angles)
        sine = jnp.sin(angles)
        new_real = jnp.dot(real_part, cosine, precision=highest) - orient * jnp.dot(
            imag_part, sine, precision=highest
        )
        new_imag = jnp.dot(imag_part, cosine, precision=highest) + orient * jnp.dot(
            real_part, sine, precision=highest
        )
        return (new_real, new_imag)
    second = length // first
    outer = real_part.shape[:-1]
    live = first
    if filled > 0 and filled % second == 0:
        live = filled // second
    real_grid = real_part.reshape(outer + (first, second))[..., :live, :]
    imag_grid = imag_part.reshape(outer + (first, second))[..., :live, :]
    counter = jnp.arange(first, dtype=jnp.int32)
    angles = (
        2.0 * math.pi / first * (counter[:, None] * counter[None, :] % first).astype(jnp.float32)
    )
    cosine = jnp.cos(angles)[:live]
    sine = jnp.sin(angles)[:live]
    section_real = jnp.einsum(
        "...ab,ak->...kb", real_grid, cosine, precision=highest
    ) - orient * jnp.einsum("...ab,ak->...kb", imag_grid, sine, precision=highest)
    section_imag = jnp.einsum(
        "...ab,ak->...kb", imag_grid, cosine, precision=highest
    ) + orient * jnp.einsum("...ab,ak->...kb", real_grid, sine, precision=highest)
    freq_rows = jnp.arange(first, dtype=jnp.int32)[:, None]
    time_cols = jnp.arange(second, dtype=jnp.int32)[None, :]
    twiddle = 2.0 * math.pi / length * (freq_rows * time_cols).astype(jnp.float32)
    twist_cos = jnp.cos(twiddle)
    twist_sin = jnp.sin(twiddle)
    turned_real = section_real * twist_cos - orient * section_imag * twist_sin
    turned_imag = section_imag * twist_cos + orient * section_real * twist_sin
    inner_real, inner_imag = transform(turned_real, turned_imag, orient, 0)
    final_real = jnp.swapaxes(inner_real, -1, -2).reshape(outer + (length,))
    final_imag = jnp.swapaxes(inner_imag, -1, -2).reshape(outer + (length,))
    return (final_real, final_imag)


def mirrored(values):
    return jnp.concatenate([values[:, :1], values[:, :0:-1]], axis=1)


def long_conv(signal, kernel):
    seq_len = signal.shape[-1]
    padded_signal = jnp.pad(signal.astype(jnp.float32), ((0, 0), (0, seq_len)))
    padded_kernel = jnp.pad(kernel, ((0, 0), (0, seq_len)))
    joint_real, joint_imag = transform(padded_signal, padded_kernel, -1.0, seq_len)
    mirror_real = mirrored(joint_real)
    mirror_imag = mirrored(joint_imag)
    signal_real = 0.5 * (joint_real + mirror_real)
    signal_imag = 0.5 * (joint_imag - mirror_imag)
    kernel_real = 0.5 * (joint_imag + mirror_imag)
    kernel_imag = -0.5 * (joint_real - mirror_real)
    prod_real = signal_real * kernel_real - signal_imag * kernel_imag
    prod_imag = signal_real * kernel_imag + signal_imag * kernel_real
    back_real, back_imag = transform(prod_real, prod_imag, 1.0, 0)
    return back_real[:, :seq_len] / (2.0 * seq_len)


def on_device(tokens, w_proj, short_filter, long_filter, skip_gain):
    rows_dev = tokens.shape[0]
    margin = short_filter.shape[1] - 1
    width = w_proj.shape[2]
    source = lax.all_gather(tokens, "mp", axis=1, tiled=True)
    projected = jnp.einsum(
        "td,dpc->tpc",
        source,
        lax.all_gather(w_proj, "seq", axis=0, tiled=True),
        preferred_element_type=jnp.float32,
    ).astype(jnp.bfloat16)
    tail = shifted(projected[rows_dev - margin :], "seq", 1)
    extended = jnp.concatenate([tail, projected], axis=0).astype(jnp.float32)
    mixed = jnp.zeros((rows_dev, 3, width), jnp.float32)
    for offset in range(margin + 1):
        mixed = (
            mixed
            + short_filter[:, offset, :][None]
            * extended[margin - offset : margin - offset + rows_dev]
        )
    query_rows = mixed[:, 0]
    product = (mixed[:, 1] * mixed[:, 2]).astype(jnp.bfloat16)
    groups = lax.axis_size("seq")
    channel_count = width // groups
    outgoing = product.reshape(rows_dev, groups, channel_count).transpose(1, 2, 0)
    arrived = lax.all_to_all(outgoing, "seq", split_axis=0, concat_axis=2, tiled=True)[0]
    convolved = long_conv(arrived, long_filter).astype(jnp.bfloat16)[None]
    returned = lax.all_to_all(convolved, "seq", split_axis=2, concat_axis=0, tiled=True)
    back_rows = returned.transpose(2, 0, 1).reshape(rows_dev, width)
    result = query_rows * (
        back_rows.astype(jnp.float32) + skip_gain[None, :] * product.astype(jnp.float32)
    )
    return result.astype(jnp.bfloat16)


def solution(mesh):
    return jax.shard_map(
        on_device,
        mesh=mesh,
        in_specs=(
            P("seq", "mp"),
            P("seq", None, "mp"),
            P(None, None, "mp"),
            P(("mp", "seq"), None),
            P("mp"),
        ),
        out_specs=P("seq", "mp"),
        check_vma=False,
    )
```

profile of v0, /device:TPU:1, one launch (start us, length us, event | category | flops | bytes accessed | tf_op | source)
XLA Modules:
  0.0 374.8 jit_solution(6726618726081883636)
XLA Ops:
  9.7 37.3 %all-gather.3.cloned.1.call-done = bf16[128,4096]{1,0:T(8,128)(2,1)} async-done(((bf16[128,1024]{1,0:T(8,128)(2,1)}), bf16[128,4096]{1,0:T(8,128)(2,1)}) %all-gather.3.cloned.1.call-update) | async-done | bytes 1048592 | tf_op jit(solution)/shard_map/all_gather | solution.py:92
  47.0 120.2 %all-gather.5.cloned.1.call-done = bf16[4096,3,512]{2,0,1:T(8,128)(2,1)} async-done(((bf16[64,3,512]{2,0,1:T(8,128)(2,1)}), bf16[4096,3,512]{2,0,1:T(8,128)(2,1)}) %all-gather.5.cloned.1.call-update) | async-done | bytes 12582928 | tf_op jit(solution)/shard_map/all_gather | solution.py:96
  167.2 6.7 %convolution_convert_fusion = bf16[128,3,512]{2,0,1:T(8,128)(2,1)S(1)} fusion(bf16[4096,3,512]{2,0,1:T(8,128)(2,1)} %all-gather.5.cloned.1.call-done, bf16[128,4096]{1,0:T(8,128)(2,1)} %all-gather.3.cloned.1.call-done), kind=kOutput, calls=%fused_computation.14 | convolution fusion | flops 1610809344 | bytes 14024704 | tf_op jit(solution)/shard_map/td,dpc->tpc/dot_general | solution.py:93
  173.9 2.8 collective-permute-start
  179.5 8.7 %all-to-all-start = ((bf16[64,8,128]{2,1,0:T(8,128)(2,1)}), bf16[64,8,128]{2,1,0:T(8,128)(2,1)S(1)}, u32[]{:S(2)}, u32[]{:S(2)}) async-start(bf16[64,8,128]{2,1,0:T(8,128)(2,1)} %bitcast.7), calls=%async_computation | async-start | bytes 262144 | tf_op jit(solution)/shard_map/all_to_all | solution.py:113
  189.1 7.4 %all-to-all-done = bf16[64,8,128]{2,1,0:T(8,128)(2,1)S(1)} async-done(((bf16[64,8,128]{2,1,0:T(8,128)(2,1)}), bf16[64,8,128]{2,1,0:T(8,128)(2,1)S(1)}, u32[]{:S(2)}, u32[]{:S(2)}) %all-to-all-start) | async-done | bytes 131104 | tf_op jit(solution)/shard_map/all_to_all | solution.py:113
  199.3 3.3 fusion.41
  203.9 1.8 copy.111
  205.7 3.3 fusion.43
  209.0 3.3 fusion.5
  212.3 4.7 %add_bitcast_fusion.1 = (f32[8,64,64,4]{1,2,3,0:T(8,128)}, f32[8,64,64,4]{1,2,3,0:T(8,128)S(1)}) fusion(f32[64,8,64,4]{2,0,3,1:T(8,128)S(1)} %fusion.5, f32[64,4]{0,1:T(4,128)S(1)} %get-tuple-element.23, f32[64,4]{0,1:T(4,128)S(1)} %get-tuple-element.22, f32[64,8,64,4]{2,0,3,1:T(8,128)S(1)} %fusion.43, f32[8,64,64,4]{2,1,3,0:T(8,128)S(1)} %copy.114), kind=kOutput, calls=%fused_computation.24 | convolution fusion | flops 101769216 | bytes 2623488 | tf_op jit(solution)/shard_map/...ab,ak->...kb/dot_general | solution.py:50
  217.3 1.9 fusion.74
  219.3 1.6 copy.120
  220.9 3.1 fusion.4
  229.1 1.9 fusion.72
  231.0 2.1 fusion.2
  234.4 8.9 %reverse = f32[8,16384]{1,0:T(8,128)S(1)} reverse(f32[8,16384]{1,0:T(8,128)S(1)} %bitcast.226), dimensions={1} | reverse | bytes 1048576
  243.5 9.3 %reverse.1 = f32[8,16384]{1,0:T(8,128)S(1)} reverse(f32[8,16384]{1,0:T(8,128)S(1)} %bitcast.229), dimensions={1} | reverse | bytes 1048576
  258.1 3.3 fusion.39
  262.8 1.8 copy.131
  264.5 3.3 fusion.45
  267.8 3.3 convolution_add_fusion
  271.1 4.6 %add_bitcast_fusion = (f32[8,64,64,4]{1,2,3,0:T(8,128)S(1)}, f32[8,64,64,4]{1,2,3,0:T(8,128)}) fusion(f32[64,8,64,4]{2,0,3,1:T(8,128)S(1)} %convolution_add_fusion, f32[64,4]{0,1:T(4,128)S(1)} %fusion.76, f32[64,4]{0,1:T(4,128)S(1)} %get-tuple-element.22, f32[64,8,64,4]{2,0,3,1:T(8,128)S(1)} %fusion.45, f32[8,64,64,4]{2,1,3,0:T(8,128)S(1)} %copy.134), kind=kOutput, calls=%fused_computation.22 | convolution fusion | flops 101638144 | bytes 2623488 | tf_op jit(solution)/shard_map/...ab,ak->...kb/dot_general | solution.py:50
  275.7 1.6 copy.139
  277.4 1.9 fusion.70
  279.7 2.0 fusion
  282.4 6.8 %copy.142 = bf16[1,8,8192]{1,0,2:T(2,128)(2,1)} copy(bf16[1,8,8192]{2,1,0:T(8,128)(2,1)S(1)} %fusion.21) | data formatting | bytes 262144 | tf_op jit(solution)/shard_map/broadcast_in_dim | solution.py:114
  289.7 45.4 %reduce = bf16[8192,8]{1,0:T(8,128)(2,1)S(1)} reduce(bf16[8192,1,8]{2,1,0:T(2,128)(2,1)} %bitcast.215, bf16[]{:T(256)} %broadcast.303), dimensions={1}, to_apply=%bitcast.180.reduce_sub_computation | reduce | bytes 262146
  335.1 2.3 reshape.159
  337.4 12.7 %all_to_all.21 = bf16[64,2,512]{2,1,0:T(2,128)(2,1)S(1)} all-to-all(bf16[64,2,512]{2,1,0:T(2,128)(2,1)S(1)} %reshape.159), channel_id=1, replica_groups=mesh['seq'=64,'mp'=4] {'seq'}, dimensions={0} | all-to-all | bytes 262144 | tf_op jit(solution)/shard_map/all_to_all | solution.py:115
  350.1 8.7 %reshape.160 = bf16[8192,1,8]{2,1,0:T(2,128)(2,1)} reshape(bf16[64,2,512]{2,1,0:T(2,128)(2,1)S(1)} %all_to_all.21) | data formatting | bytes 262144
  358.8 7.8 %copy.143 = bf16[1,8,8192]{2,1,0:T(8,128)(2,1)S(1)} copy(bf16[1,8,8192]{1,0,2:T(2,128)(2,1)} %bitcast.216) | data formatting | bytes 262144 | tf_op jit(solution)/shard_map/all_to_all | solution.py:115
  (74 shorter events, 27.1 us)
Async XLA Ops:
  6.5 181.7 %copy-start.3 = (f32[8,8192]{1,0:T(8,128)S(1)}, f32[8,8192]{1,0:T(8,128)}, u32[]{:S(2)}) copy-start(f32[8,8192]{1,0:T(8,128)} %param.8) | copy-start | bytes 786436
  6.5 40.4 %all-gather.3.cloned.1.call-start = ((), (), s32[]{:S(2)}) async-start(), calls=%async_computation.2 | async-start | bytes 1310720 | tf_op jit(solution)/shard_map/all_gather | solution.py:92
  7.3 159.9 %all-gather.5.cloned.1.call-start = ((), (), s32[]{:S(2)}) async-start(), calls=%async_computation.3 | async-start | bytes 12779520 | tf_op jit(solution)/shard_map/all_gather | solution.py:96
  173.9 3.6 collective-permute-start
  177.8 0.9 copy-start
  179.5 17.0 %all-to-all-start = ((bf16[64,8,128]{2,1,0:T(8,128)(2,1)}), bf16[64,8,128]{2,1,0:T(8,128)(2,1)S(1)}, u32[]{:S(2)}, u32[]{:S(2)}) async-start(bf16[64,8,128]{2,1,0:T(8,128)(2,1)} %bitcast.7), calls=%async_computation | async-start | bytes 262144 | tf_op jit(solution)/shard_map/all_to_all | solution.py:113
  227.8 25.2 %slice-start = ((f32[8,16384]{1,0:T(8,128)}), f32[8,1]{1,0:T(8,128)S(1)}, s32[]{:S(2)}) async-start(f32[8,16384]{1,0:T(8,128)} %reshape.130), calls=%async_computation.4 | async-start | bytes 8192 | tf_op jit(solution)/shard_map/slice | solution.py:68
  227.8 25.6 %copy-start.2 = (f32[8,64,256]{2,1,0:T(8,128)S(1)}, f32[8,64,256]{2,1,0:T(8,128)}, u32[]{:S(2)}) copy-start(f32[8,64,256]{2,1,0:T(8,128)} %reshape.129) | copy-start | bytes 1572868
  282.0 85.0 %copy-start.1 = (f32[128,3,512]{2,0,1:T(8,128)S(1)}, f32[128,3,512]{2,0,1:T(8,128)}, u32[]{:S(2)}) copy-start(f32[128,3,512]{2,0,1:T(8,128)} %copy-done) | copy-start | bytes 2359300
  282.0 85.0 %copy-start.4 = (f32[512]{0:T(512)S(1)}, f32[512]{0:T(512)}, u32[]{:S(2)}) copy-start(f32[512]{0:T(512)} %param.9) | copy-start | bytes 6148
Sparse Core Ops, SparseCore 0:
  9.1 37.7 all-gather.2
  48.8 118.2 all-gather.4
where the time goes:
time: 379 us; the launch traced here: 375 us
  waiting for transfers between devices  167 us (44%)
  local copies, waits for them, and re-layouts  67.2 us (18%)
  matrix products  54 us (14%)
  other arithmetic  48.3 us (13%)
  between operations  14.1 us (4%)
  blocking collectives  12.7 us (3%)
  starting transfers between devices  11.5 us (3%)
    all_gather x1, waiting for transfers between devices, on_device(): lax.all_gather(w_proj, 'seq', axis=0, tiled=True)  120 us
    unnamed x2, other arithmetic  45.4 us
    all_gather x1, waiting for transfers between devices, on_device(): source = lax.all_gather(tokens, 'mp', axis=1, tiled=True)  37.3 us
    unnamed x22, local copies, waits for them, and re-layouts  31.3 us
    all_to_all x1, blocking collectives, on_device(): lax.all_to_all(convolved, 'seq', split_axis=2, concat_axis=0, tiled=True)  12.7 us
    dot_general x4, matrix products, transform(): jnp.einsum('...ab,ak->...kb', imag_grid, sine, precision=highest)  10.8 us
    all_to_all x1, starting transfers between devices, on_device(): lax.all_to_all(outgoing, 'seq', split_axis=0, concat_axis=2, tiled=True)[0]  8.66 us
    dot_general x4, matrix products, transform(): jnp.einsum('...ab,ak->...kb', imag_grid, cosine, precision=highest)  7.92 us
  transfers between devices with their start and end apart: 4, of which 4 were waited for; matrix products, arithmetic and copies ran while one was open for 1% of the time, Pallas kernels for 0%

commit v1 on v0

--- a/solution.py
+++ b/solution.py
@@ -112,7 +112,10 @@
     outgoing = product.reshape(rows_dev, groups, channel_count).transpose(1, 2, 0)
     arrived = lax.all_to_all(outgoing, "seq", split_axis=0, concat_axis=2, tiled=True)[0]
     convolved = long_conv(arrived, long_filter).astype(jnp.bfloat16)[None]
-    returned = lax.all_to_all(convolved, "seq", split_axis=2, concat_axis=0, tiled=True)
+    returned = jnp.concatenate(
+        lax.all_to_all(jnp.stack(jnp.split(convolved, lax.axis_size("seq"), axis=2)), "seq", 0, 0),
+        axis=0,
+    )
     back_rows = returned.transpose(2, 0, 1).reshape(rows_dev, width)
     result = query_rows * (
         back_rows.astype(jnp.float32) + skip_gain[None, :] * product.astype(jnp.float32)

time: 379 us -> 355 us (0.937)
  other arithmetic: 48.3 us -> 2.9 us
  local copies, waits for them, and re-layouts: 67.2 us -> 79.6 us
  matrix products: 54 us -> 60.9 us
    unnamed x2 -> x0, other arithmetic: 45.4 us -> none
    unnamed x22 -> x77, local copies, waits for them, and re-layouts: 31.3 us -> 58.2 us
    all_to_all x1 -> x0, local copies, waits for them, and re-layouts: 7.79 us -> none  [on_device(): lax.all_to_all(convolved, 'seq', split_axis=2, concat_axis=0, tiled=True)]
    broadcast_in_dim x1 -> x0, local copies, waits for them, and re-layouts: 6.75 us -> none  [on_device(): convolved = long_conv(arrived, long_filter).astype(jnp.bfloat16)[None]]
where the time goes in v1:
time: 355 us; the launch traced here: 349 us
  waiting for transfers between devices  167 us (47%)
  local copies, waits for them, and re-layouts  79.6 us (22%)
  matrix products  60.9 us (17%)
  between operations  14.2 us (4%)
  blocking collectives  12.7 us (4%)
  starting transfers between devices  11.5 us (3%)
    all_gather x1, waiting for transfers between devices, on_device(): lax.all_gather(w_proj, 'seq', axis=0, tiled=True)  120 us
    unnamed x77, local copies, waits for them, and re-layouts  58.2 us
    all_gather x1, waiting for transfers between devices, on_device(): source = lax.all_gather(tokens, 'mp', axis=1, tiled=True)  37.3 us
    dot_general x4, matrix products, transform(): jnp.einsum('...ab,ak->...kb', imag_grid, sine, precision=highest)  13.4 us
    all_to_all x1, blocking collectives, on_device(): lax.all_to_all(jnp.stack(jnp.split(convolved, lax.axis_size('seq'), axis=...  12.7 us
    dot_general x4, matrix products, transform(): jnp.einsum('...ab,ak->...kb', real_grid, cosine, precision=highest)  9.83 us
    all_to_all x1, starting transfers between devices, on_device(): lax.all_to_all(outgoing, 'seq', split_axis=0, concat_axis=2, tiled=True)[0]  8.67 us
    dot_general x4, matrix products, transform(): jnp.einsum('...ab,ak->...kb', imag_grid, cosine, precision=highest)  7.92 us
  transfers between devices with their start and end apart: 4, of which 4 were waited for; matrix products, arithmetic and copies ran while one was open for 1% of the time, Pallas kernels for 0%

profile of v1, /device:TPU:1, one launch (start us, length us, event | category | flops | bytes accessed | tf_op | source)
XLA Modules:
  0.0 348.8 jit_solution(6762061076999726116)
XLA Ops:
  9.7 37.3 %all-gather.3.cloned.1.call-done = bf16[128,4096]{1,0:T(8,128)(2,1)} async-done(((bf16[128,1024]{1,0:T(8,128)(2,1)}), bf16[128,4096]{1,0:T(8,128)(2,1)}) %all-gather.3.cloned.1.call-update) | async-done | bytes 1048592 | tf_op jit(solution)/shard_map/all_gather | solution.py:92
  47.0 120.2 %all-gather.5.cloned.1.call-done = bf16[4096,3,512]{2,0,1:T(8,128)(2,1)} async-done(((bf16[64,3,512]{2,0,1:T(8,128)(2,1)}), bf16[4096,3,512]{2,0,1:T(8,128)(2,1)}) %all-gather.5.cloned.1.call-update) | async-done | bytes 12582928 | tf_op jit(solution)/shard_map/all_gather | solution.py:96
  167.2 6.7 %convolution_convert_fusion = bf16[128,3,512]{2,0,1:T(8,128)(2,1)S(1)} fusion(bf16[4096,3,512]{2,0,1:T(8,128)(2,1)} %all-gather.5.cloned.1.call-done, bf16[128,4096]{1,0:T(8,128)(2,1)} %all-gather.3.cloned.1.call-done), kind=kOutput, calls=%fused_computation.14 | convolution fusion | flops 1610809344 | bytes 14024704 | tf_op jit(solution)/shard_map/td,dpc->tpc/dot_general | solution.py:93
  173.9 2.8 collective-permute-start
  178.7 8.7 %all-to-all-start = ((bf16[64,8,128]{2,1,0:T(8,128)(2,1)}), bf16[64,8,128]{2,1,0:T(8,128)(2,1)S(1)}, u32[]{:S(2)}, u32[]{:S(2)}) async-start(bf16[64,8,128]{2,1,0:T(8,128)(2,1)} %bitcast.7), calls=%async_computation | async-start | bytes 262144 | tf_op jit(solution)/shard_map/all_to_all | solution.py:113
  188.2 7.4 %all-to-all-done = bf16[64,8,128]{2,1,0:T(8,128)(2,1)S(1)} async-done(((bf16[64,8,128]{2,1,0:T(8,128)(2,1)}), bf16[64,8,128]{2,1,0:T(8,128)(2,1)S(1)}, u32[]{:S(2)}, u32[]{:S(2)}) %all-to-all-start) | async-done | bytes 131104 | tf_op jit(solution)/shard_map/all_to_all | solution.py:113
  198.4 4.3 %fusion.43 = f32[64,8,64,4]{2,0,3,1:T(8,128)} fusion(f32[8,64,64,4]{2,1,3,0:T(8,128)S(1)} %copy.136), kind=kOutput, calls=%fused_computation.152 | convolution fusion | flops 100720640 | bytes 1048576 | tf_op jit(solution)/shard_map/...ab,ak->...kb/dot_general | solution.py:48
  202.7 1.3 copy.137
  204.0 1.8 copy.139
  205.8 3.3 fusion.41
  209.1 3.3 fusion.5
  212.3 5.8 %add_bitcast_fusion.1 = (f32[8,64,64,4]{1,2,3,0:T(8,128)S(1)}, f32[8,64,64,4]{1,2,3,0:T(8,128)}) fusion(f32[64,8,64,4]{2,0,3,1:T(8,128)S(1)} %fusion.5, f32[64,4]{0,1:T(4,128)S(1)} %get-tuple-element.23, f32[64,4]{0,1:T(4,128)S(1)} %get-tuple-element.22, f32[64,8,64,4]{2,0,3,1:T(8,128)} %fusion.43, f32[8,64,64,4]{2,1,3,0:T(8,128)S(1)} %copy.139), kind=kOutput, calls=%fused_computation.24 | convolution fusion | flops 101769216 | bytes 2623488 | tf_op jit(solution)/shard_map/...ab,ak->...kb/dot_general | solution.py:50
  218.6 1.6 copy.144
  220.2 1.9 fusion.74
  222.1 2.9 fusion.72
  225.1 3.1 fusion.4
  228.2 1.5 copy.188
  230.1 1.1 reshape.130
  232.2 3.3 fusion.2
  236.8 47.7 %reverse = f32[8,16384]{1,0:T(8,128)S(1)} reverse(f32[8,16384]{1,0:T(8,128)} %bitcast.469), dimensions={1} | reverse | bytes 1048576
  284.7 9.3 %reverse.1 = f32[8,16384]{1,0:T(8,128)S(1)} reverse(f32[8,16384]{1,0:T(8,128)S(1)} %bitcast.470), dimensions={1} | reverse | bytes 1048576
  299.3 4.3 %fusion.45 = f32[64,8,64,4]{2,0,3,1:T(8,128)} fusion(f32[8,64,64,4]{2,1,3,0:T(8,128)S(1)} %copy.156), kind=kOutput, calls=%fused_computation.154 | convolution fusion | flops 100720640 | bytes 1048576 | tf_op jit(solution)/shard_map/...ab,ak->...kb/dot_general | solution.py:48
  303.6 1.3 copy.157
  304.9 1.8 copy.159
  306.7 3.3 fusion.39
  310.0 3.3 convolution_add_fusion
  313.3 6.1 %add_bitcast_fusion = (f32[8,64,64,4]{1,2,3,0:T(8,128)}, f32[8,64,64,4]{1,2,3,0:T(8,128)}) fusion(f32[64,8,64,4]{2,0,3,1:T(8,128)S(1)} %convolution_add_fusion, f32[64,4]{0,1:T(4,128)S(1)} %fusion.76, f32[64,4]{0,1:T(4,128)S(1)} %get-tuple-element.22, f32[64,8,64,4]{2,0,3,1:T(8,128)} %fusion.45, f32[8,64,64,4]{2,1,3,0:T(8,128)S(1)} %copy.159), kind=kOutput, calls=%fused_computation.22 | convolution fusion | flops 101638144 | bytes 2623488 | tf_op jit(solution)/shard_map/...ab,ak->...kb/dot_general | solution.py:50
  319.4 1.6 copy.165
  321.0 1.6 copy.164
  322.7 1.9 fusion.70
  324.6 2.1 fusion
  328.2 12.7 %all_to_all.14 = bf16[64,1,8,128]{3,2,1,0:T(8,128)(2,1)S(1)} all-to-all(bf16[64,1,8,128]{3,2,1,0:T(8,128)(2,1)S(1)} %constant_dynamic-update-slice_fusion), channel_id=1, replica_groups=mesh['seq'=64,'mp'=4] {'seq'}, dimensions={0} | all-to-all | bytes 262144 | tf_op jit(solution)/shard_map/all_to_all | solution.py:116
  (125 shorter events, 19.2 us)
Async XLA Ops:
  6.5 180.8 %copy-start.1 = (f32[8,8192]{1,0:T(8,128)S(1)}, f32[8,8192]{1,0:T(8,128)}, u32[]{:S(2)}) copy-start(f32[8,8192]{1,0:T(8,128)} %param.8) | copy-start | bytes 786436
  6.5 40.4 %all-gather.3.cloned.1.call-start = ((), (), s32[]{:S(2)}) async-start(), calls=%async_computation.2 | async-start | bytes 1310720 | tf_op jit(solution)/shard_map/all_gather | solution.py:92
  7.3 159.9 %all-gather.5.cloned.1.call-start = ((), (), s32[]{:S(2)}) async-start(), calls=%async_computation.3 | async-start | bytes 12779520 | tf_op jit(solution)/shard_map/all_gather | solution.py:96
  173.9 3.6 %collective-permute-start = (bf16[2,3,512]{2,0,1:T(2,128)(2,1)S(1)}, bf16[2,3,512]{2,0,1:T(2,128)(2,1)S(1)}, u32[]{:S(2)}, u32[]{:S(2)}) collective-permute-start(bf16[2,3,512]{2,0,1:T(2,128)(2,1)S(1)} %slice.84), channel_id=1, source_target_pairs={{0,4},{4,8},{8,12},{12,16},{16,20},{20,24},{24,28},{28,32},{32,36}... | collective-permute-start | bytes 18440 | tf_op jit(solution)/shard_map/ppermute | solution.py:11
  178.7 17.0 %all-to-all-start = ((bf16[64,8,128]{2,1,0:T(8,128)(2,1)}), bf16[64,8,128]{2,1,0:T(8,128)(2,1)S(1)}, u32[]{:S(2)}, u32[]{:S(2)}) async-start(bf16[64,8,128]{2,1,0:T(8,128)(2,1)} %bitcast.7), calls=%async_computation | async-start | bytes 262144 | tf_op jit(solution)/shard_map/all_to_all | solution.py:113
  232.2 62.4 %copy-start = (f32[8,64,256]{2,1,0:T(8,128)S(1)}, f32[8,64,256]{2,1,0:T(8,128)}, u32[]{:S(2)}) copy-start(f32[8,64,256]{2,1,0:T(8,128)} %reshape.130) | copy-start | bytes 1572868
  306.7 34.3 %copy-start.2 = (f32[512]{0:T(512)S(1)}, f32[512]{0:T(512)}, u32[]{:S(2)}) copy-start(f32[512]{0:T(512)} %param.9) | copy-start | bytes 6148
Sparse Core Ops, SparseCore 0:
  9.1 37.7 all-gather.2
  48.8 118.2 all-gather.4
